TPU v7x, 256 devices: a whole 4x4x8 slice. The times are simulated.
256 devices in a mesh: ctx: 32 (over y, x, core), head: 8 (over z).
Axes of the slice: x: 4, y: 4, z: 8, core: 2. Of those that a mesh axis runs over, the one named last changes fastest.
Arguments:
- ssm_input: bfloat16 [8192, 8192], P('ctx', 'head'), may hold values from -6 to 6
- gate_input: bfloat16 [8192, 8192], P('ctx', 'head'), may hold values from -6 to 6
- step_raw: float32 [8192, 128], P('ctx', 'head'), may hold values from -4 to 4
- b_matrix: bfloat16 [8192, 1024], P('ctx', 'head'), may hold values from -6 to 6
- c_matrix: bfloat16 [8192, 1024], P('ctx', 'head'), may hold values from -6 to 6
- step_bias: float32 [128], P('head'), may hold values from -6 to -4
- log_rate: float32 [128], P('head')
- skip_gain: float32 [128], P('head'), may hold values from 0.5 to 1.5
- norm_weight: float32 [8192], P('head'), may hold values from 0.5 to 1.5
- doc_resets: int32 [8192], P('ctx'), may hold values from 0 to 1, as said below
- grad_output: bfloat16 [8192, 8192], P('ctx', 'head'), may hold values from -6 to 6
Outputs:
- grad_input: bfloat16 [8192, 8192], P('ctx', 'head')
- grad_gate: bfloat16 [8192, 8192], P('ctx', 'head')
- grad_step: float32 [8192, 128], P('ctx', 'head')
- grad_b_matrix: float32 [8192, 1024], P('ctx', 'head')
- grad_c_matrix: float32 [8192, 1024], P('ctx', 'head')
Inputs may be any that keep to these rules, and one draw needn't show every extreme that they name: `doc_resets`: exactly 4 positions hold 1, all of them among positions 1 to 127; all others hold 0.
All inputs are finite; a program needn't handle non-finite values.
Results may differ from a plain program's by a relative error of at most 0.001.
Values sent between devices are 32-bit elements; how exact they have to be, the bound alone decides.
No kernel may reach another device: no remote copies, remote signals or barrier semaphores. Data moves between devices by JAX's collectives and lax.ppermute only.
A program may use at most 64 MiB of HBM per device.

v0:
```python
import jax
import jax.numpy as jnp
from jax import lax
from jax.sharding import PartitionSpec as P

HEAD_DIM = 64
STATE = 128
SPAN = 256
HIGHEST_PRECISION = lax.Precision.HIGHEST
EPSILON = 1e-05


def carried_in(array, axis, combine, identity):
    size, index = (lax.axis_size(axis), lax.axis_index(axis))
    everything = jax.tree.map(lambda part: lax.all_gather(part, axis), array)
    start = jax.tree.map(
        lambda part, zero: jnp.broadcast_to(jnp.asarray(zero, part.dtype), part.shape),
        array,
        identity,
    )

    def turn(k, before):
        at = size - 1 - k
        reached = at > index
        new = combine(before, jax.tree.map(lambda part: part[at], everything))
        return jax.tree.map(lambda a, b: jnp.where(reached, a, b), new, before)

    return lax.fori_loop(0, size, turn, start)


def span_mix(x_span, dt_span, b_span, c_span, log_cum, segment):
    log_rows = jnp.moveaxis(log_cum, 0, -1)
    spread = log_rows[..., :, None] - log_rows[..., None, :]
    places = jnp.arange(x_span.shape[0], dtype=jnp.int32)
    keep_mask = (
        (places[:, None] >= places[None, :]) & (segment[:, None] == segment[None, :])
    ).astype(jnp.float32)
    masked = jnp.exp(jnp.minimum(spread, 0.0)) * keep_mask
    scores = jnp.einsum("tgn,sgn->gts", c_span, b_span, precision=HIGHEST_PRECISION)
    weights = scores[:, None] * masked * jnp.moveaxis(dt_span, 0, -1)[..., None, :]
    return jnp.einsum("ghts,sghp->tghp", weights, x_span, precision=HIGHEST_PRECISION)


def block_decays(dt_spans, segment, decay_rate):
    log_cum = jnp.cumsum(dt_spans * decay_rate, axis=1)
    closing = segment[:, -1]
    through = jnp.exp(log_cum[:, -1]) * (closing == 0).astype(jnp.float32)[:, None, None]
    return (log_cum, closing, through)


def local_states(x_spans, dt_spans, b_spans, segment, decay_rate):
    log_cum, closing, through = block_decays(dt_spans, segment, decay_rate)
    same_doc = (segment == closing[:, None]).astype(jnp.float32)
    tail_decay = jnp.exp(log_cum[:, -1:] - log_cum) * same_doc[:, :, None, None]
    added_terms = jnp.einsum(
        "kqgh,kqghp,kqgn->kghpn",
        tail_decay * dt_spans,
        x_spans,
        b_spans,
        precision=HIGHEST_PRECISION,
    )

    def advance(carried_pair, item_pair):
        carry_state, product = carried_pair
        decay_now, fresh_state = item_pair
        return (
            (decay_now[..., None, None] * carry_state + fresh_state, product * decay_now),
            carry_state,
        )

    initial = (
        jnp.zeros(added_terms.shape[1:], jnp.float32),
        jnp.ones(through.shape[1:], jnp.float32),
    )
    (final_state, product), starts = lax.scan(advance, initial, (through, added_terms))
    return (starts, final_state, product)


def output_part(x_spans, dt_spans, b_spans, c_spans, segment, decay_rate, starts, entry_state):
    log_cum, closing, through = block_decays(dt_spans, segment, decay_rate)

    def rolling(product, decay_now):
        return (product * decay_now, product)

    _, before = lax.scan(rolling, jnp.ones(through.shape[1:], jnp.float32), through)
    full_start = starts + before[..., None, None] * entry_state[None]
    opened = (segment == 0).astype(jnp.float32)
    entry_decay = jnp.exp(log_cum) * opened[:, :, None, None]
    carried = (
        jnp.einsum("kqgn,kghpn->kqghp", c_spans, full_start, precision=HIGHEST_PRECISION)
        * entry_decay[..., None]
    )
    mix_block = jax.checkpoint(lambda pieces: span_mix(*pieces))
    inner_part = lax.map(mix_block, (x_spans, dt_spans, b_spans, c_spans, log_cum, segment))
    return inner_part + carried


def compose(earlier, later):
    decay_early, sum_early = earlier
    decay_late, sum_late = later
    return (decay_early * decay_late, decay_late[..., None, None] * sum_early + sum_late)


def body(
    ssm_input,
    gate_input,
    step_raw,
    b_matrix,
    c_matrix,
    step_bias,
    log_rate,
    skip_gain,
    norm_weight,
    doc_resets,
    grad_output,
):
    tokens_here = ssm_input.shape[0]
    heads_here = step_raw.shape[1]
    groups_here = b_matrix.shape[1] // STATE
    per_group = heads_here // groups_here
    spans = tokens_here // SPAN
    x_float = ssm_input.astype(jnp.float32)
    gate_float = gate_input.astype(jnp.float32)
    shifted = step_raw + step_bias[None, :]
    step_size = jax.nn.softplus(shifted)
    decay_rate = (-jnp.exp(log_rate)).reshape(groups_here, per_group)
    x_spans = x_float.reshape(spans, SPAN, groups_here, per_group, HEAD_DIM)
    dt_spans = step_size.reshape(spans, SPAN, groups_here, per_group)
    b_spans = b_matrix.astype(jnp.float32).reshape(spans, SPAN, groups_here, STATE)
    c_spans = c_matrix.astype(jnp.float32).reshape(spans, SPAN, groups_here, STATE)
    segment = jnp.cumsum(doc_resets.reshape(spans, SPAN), axis=1, dtype=jnp.int32)

    def states_call(x_value, dt_value, b_value):
        return local_states(x_value, dt_value, b_value, segment, decay_rate)

    (starts, end_local, through_all), states_back = jax.vjp(states_call, x_spans, dt_spans, b_spans)
    identity = (jnp.ones_like(through_all), jnp.zeros_like(end_local))
    decay_table = lax.all_gather(through_all, "ctx", axis=0, tiled=True)
    own_index = lax.axis_index("ctx")
    ctx_count = lax.axis_size("ctx")
    flat_end = end_local.reshape(heads_here, HEAD_DIM, STATE)
    row_ids = jnp.arange(lax.axis_size("ctx") * heads_here, dtype=jnp.int32)
    receiver = row_ids // heads_here
    head_ids = row_ids % heads_here
    devices = jnp.arange(ctx_count, dtype=jnp.int32)
    between = (devices[None, :] > own_index) & (devices[None, :] < receiver[:, None])
    factors = jnp.where(between, decay_table[:, head_ids].T, 1.0)
    weight = jnp.prod(factors, axis=1) * (own_index < receiver).astype(jnp.float32)
    entry_state = lax.psum_scatter(
        weight[:, None, None] * jnp.take(flat_end, head_ids, axis=0),
        "ctx",
        scatter_dimension=0,
        tiled=True,
    ).reshape(end_local.shape)

    def output_call(x_value, dt_value, b_value, c_value, start_value, entry_value):
        return output_part(
            x_value, dt_value, b_value, c_value, segment, decay_rate, start_value, entry_value
        )

    core_part, output_back = jax.vjp(
        output_call, x_spans, dt_spans, b_spans, c_spans, starts, entry_state
    )
    skip_cols = jnp.repeat(skip_gain, HEAD_DIM)[None, :]
    core_out = core_part.reshape(tokens_here, heads_here * HEAD_DIM) + x_float * skip_cols
    gate_sig = jax.nn.sigmoid(gate_float)
    gate_act = gate_float * gate_sig
    gated = core_out * gate_act
    weighted_grad = norm_weight[None, :] * grad_output.astype(jnp.float32)
    norm_width = lax.axis_size("head") * gated.shape[1]
    squares = lax.psum(jnp.sum(gated * gated, axis=1), "head")
    inv_rms = lax.rsqrt(squares / norm_width + EPSILON)
    normed = gated * inv_rms[:, None]
    product = lax.psum(jnp.sum(weighted_grad * normed, axis=1), "head")
    grad_gated = inv_rms[:, None] * (weighted_grad - normed * (product / norm_width)[:, None])
    grad_core = grad_gated * gate_act
    grad_gate = grad_gated * core_out * gate_sig * (1.0 + gate_float * (1.0 - gate_sig))
    first_grads = output_back(grad_core.reshape(core_part.shape))
    _, exit_adjoint = carried_in((through_all, first_grads[5]), "ctx", compose, identity)
    through_grad = jnp.sum(exit_adjoint * entry_state, axis=(2, 3))
    second_grads = states_back((first_grads[4], exit_adjoint, through_grad))
    grad_input = (first_grads[0] + second_grads[0]).reshape(
        tokens_here, heads_here * HEAD_DIM
    ) + grad_core * skip_cols
    grad_step = (first_grads[1] + second_grads[1]).reshape(
        tokens_here, heads_here
    ) * jax.nn.sigmoid(shifted)
    grad_b_matrix = (first_grads[2] + second_grads[2]).reshape(tokens_here, groups_here * STATE)
    grad_c_matrix = first_grads[3].reshape(tokens_here, groups_here * STATE)
    return (
        grad_input.astype(jnp.bfloat16),
        grad_gate.astype(jnp.bfloat16),
        grad_step,
        grad_b_matrix,
        grad_c_matrix,
    )


def solution(mesh):
    return jax.shard_map(
        body,
        mesh=mesh,
        in_specs=(
            P("ctx", "head"),
            P("ctx", "head"),
            P("ctx", "head"),
            P("ctx", "head"),
            P("ctx", "head"),
            P("head"),
            P("head"),
            P("head"),
            P("head"),
            P("ctx"),
            P("ctx", "head"),
        ),
        out_specs=(
            P("ctx", "head"),
            P("ctx", "head"),
            P("ctx", "head"),
            P("ctx", "head"),
            P("ctx", "head"),
        ),
        check_vma=False,
    )
```

profile of v0, /device:TPU:1, one launch (start us, length us, event | category | flops | bytes accessed | tf_op | source)
XLA Modules:
  0.0 404.8 jit_solution(4905228115888977162)
XLA Ops:
  14.6 1.3 copy.242
  15.8 23.2 %all-gather = f32[32,1,1,16]{3,2,1,0:T(1,128)S(1)} all-gather(f32[1,1,1,16]{3,2,1,0:T(1,128)S(1)} %get-tuple-element.418), channel_id=2, replica_groups=mesh['ctx'=32,'head'=8] {'ctx'}, dimensions={0}, use_global_device_ids=true | all-gather | bytes 2112 | tf_op jit(solution)/shard_map/all_gather | solution.py:138
  39.1 1.5 fusion.46
  40.6 7.0 %gather_fusion.1 = f32[512,64,128]{2,1,0:T(8,128)} fusion(f32[16,64,128]{2,1,0:T(8,128)S(1)} %fusion.46, s32[1024]{0:T(1024)S(1)} %pad_clamp_fusion), kind=kCustom, calls=%fused_computation.1 | custom fusion | bytes 33556480 | tf_op jit(solution)/shard_map/jit(_take)/gather | solution.py:150
  47.6 1.0 gather_fusion
  48.9 11.9 %select_multiply_fusion = f32[512,64,128]{2,1,0:T(8,128)} fusion(f32[512,64,128]{2,1,0:T(8,128)} %gather_fusion.1, f32[512]{0:T(512)S(1)} %compare_select_fusion.3, pred[512]{0:T(512)(128)(4,1)S(1)} %compare_and_fusion), kind=kLoop, calls=%fused_computation.5 | loop fusion | flops 8388608 | bytes 33556992 | tf_op jit(solution)/shard_map/mul | solution.py:150
  62.6 120.6 %reduce-scatter.2.cloned.1.call-done = f32[16,64,128]{2,1,0:T(8,128)} async-done(((f32[512,64,128]{2,1,0:T(8,128)}), f32[16,64,128]{2,1,0:T(8,128)}) %reduce-scatter.2.cloned.1.call-update) | async-done | bytes 524304 | tf_op jit(solution)/shard_map/reduce_scatter | solution.py:149
  183.2 1.6 convolution_bitcast_fusion.1
  184.9 3.2 fusion.38
  189.1 14.0 %psum.14 = f32[256]{0:T(256)S(1)} all-reduce(f32[256]{0:T(256)S(1)} %get-tuple-element.406), channel_id=1, replica_groups=mesh['ctx'=32,'head'=8] {'head'}, use_global_device_ids=true, to_apply=%region_7.8 | all-reduce | flops 256 | bytes 2048 | tf_op jit(solution)/shard_map/psum | solution.py:171
  203.4 11.2 %psum.15 = f32[256]{0:T(256)S(1)} all-reduce(f32[256]{0:T(256)S(1)} %multiply_reduce_fusion.1), channel_id=1, replica_groups=mesh['ctx'=32,'head'=8] {'head'}, use_global_device_ids=true, to_apply=%region_9.10 | all-reduce | flops 256 | bytes 2048 | tf_op jit(solution)/shard_map/psum | solution.py:174
  214.6 3.0 fusion.56
  217.6 1.4 fusion.58
  219.0 1.1 convert.11
  221.0 2.0 multiply_reduce_fusion
  223.0 1.5 copy.259
  224.4 1.0 copy.279
  225.4 3.2 convolution_bitcast_fusion.3
  228.6 74.7 %all-gather.5.cloned.1.call-done = f32[512,64,128]{2,1,0:T(8,128)} async-done(((f32[16,64,128]{2,1,0:T(8,128)}), f32[512,64,128]{2,1,0:T(8,128)}) %all-gather.5.cloned.1.call-update) | async-done | bytes 16777232 | tf_op jit(solution)/shard_map/all_gather | solution.py:15
  303.4 59.4 %while.11 = (s32[]{:T(128)}, f32[1,16,64,128]{3,2,1,0:T(8,128)S(1)}, s32[]{:T(128)}, f32[32,1,16]{2,1,0:T(1,128)}, f32[32,1,16,64,128]{4,3,2,1,0:T(8,128)}, /*index=5*/s32[]{:T(128)}, s32[]{:T(128)}, s32[]{:T(128)}, s32[]{:T(128)}) while((s32[]{:T(128)}, f32[1,16,64,128]{3,2,1,0:T(8,128)S(1)}, s32[]{:T(128)}, ...), condition=%wide.region_11.12_spmd.clone, body=%wide.region_10.11_spmd.clone.sunk | while | flops 524296 | bytes 1573223 | solution.py:28
  304.1 1.2 fusion.115
  305.9 1.2 fusion.115
  307.8 1.2 fusion.115
  309.6 1.2 fusion.115
  311.5 1.2 fusion.115
  313.3 1.2 fusion.115
  315.2 1.2 fusion.115
  317.0 1.2 fusion.115
  318.9 1.2 fusion.115
  320.8 1.2 fusion.115
  322.6 1.2 fusion.115
  324.5 1.2 fusion.115
  326.3 1.2 fusion.115
  328.2 1.2 fusion.115
  330.0 1.2 fusion.115
  331.9 1.2 fusion.115
  333.7 1.2 fusion.115
  335.6 1.2 fusion.115
  337.4 1.2 fusion.115
  339.3 1.2 fusion.115
  341.2 1.2 fusion.115
  343.0 1.2 fusion.115
  344.9 1.2 fusion.115
  346.7 1.2 fusion.115
  348.6 1.2 fusion.115
  350.4 1.2 fusion.115
  352.3 1.2 fusion.115
  354.1 1.2 fusion.115
  356.0 1.2 fusion.115
  357.8 1.2 fusion.115
  359.7 1.2 fusion.115
  361.6 1.2 fusion.115
  362.8 1.6 fusion.50
  364.4 1.8 fusion.47
  366.9 8.3 %fusion.77 = (f32[16,256]{1,0:T(8,128)S(1)}, f32[16,256]{1,0:T(8,128)S(1)}, f32[16,256]{1,0:T(8,128)}, f32[256,256]{1,0:T(8,128)S(1)}) fusion(f32[16,256]{1,0:T(8,128)S(1)} %bitcast.277, f32[256,256]{1,0:T(8,128)S(1)} %fusion.81, f32[16,256]{1,0:T(8,128)S(1)} %bitcast.279, f32[256,256]{1,0:T(8,128)S(1)} %fusion.85, f32[256,1,16,64]{0,3,2,1:T(8,128)S(1)} %copy-done.8, ...), kind=kOutput, calls=%fused_computation.95 | convolution fusion | flops 825151488 | bytes 2965504 | tf_op jit(solution)/shard_map/transpose(jvp())/while/body/eval_jaxpr/checkpoint/ghts,sghp->tghp/dot_general | solution.py:41
  376.3 1.4 pad_add_fusion.1
  378.7 2.5 reduce-window.36
  381.3 2.7 reduce-window.34
  384.1 1.9 convolution_add_fusion
  386.1 1.2 fusion.49
  389.3 1.1 fusion.83
  390.5 1.4 bitcast_multiply_fusion.1
  391.9 4.8 %fusion.41 = f32[256,16,64]{0,2,1:T(8,128)S(1)} fusion(f32[16,256]{1,0:T(8,128)} %bitcast.280, f32[256,256]{1,0:T(8,128)} %copy-done.13, f32[16,256]{1,0:T(8,128)} %bitcast.276, f32[256,256]{1,0:T(8,128)} %copy-done.14, f32[256,1,16,64]{0,3,2,1:T(8,128)S(1)} %bitcast.251, f32[256,16,64]{0,2,1:T(8,128)S(1)} %copy-done.9, f32[256,16]{0,1:T(8,128)S(1)} %bitcast.264), kind=kOutput, calls=%fused_computation.47 | convolution fusion | flops 811073536 | bytes 3719168 | tf_op jit(solution)/shard_map/transpose(jvp())/while/body/eval_jaxpr/checkpoint/ghts,sghp->tghp/dot_general | solution.py:41
  397.0 1.0 copy.278
  (179 shorter events, 36.4 us)
Async XLA Ops:
  7.2 176.0 %reduce-scatter.2.cloned.1.call-start = ((), (), s32[]{:S(2)}) async-start(), calls=%async_computation.1 | async-start | bytes 17301504 | tf_op jit(solution)/shard_map/reduce_scatter | solution.py:149
  7.9 0.8 copy-start.32
  10.9 3.1 copy-start.30
  10.9 51.4 %copy-start.21 = (s32[256]{0:T(256)}, s32[256]{0:T(256)S(1)}, u32[]{:S(2)}) copy-start(s32[256]{0:T(256)S(1)} %get-tuple-element.298) | copy-start | bytes 3076
  14.0 33.6 %copy-start.29 = (f32[16]{0:T(128)}, f32[16]{0:T(128)S(1)}, u32[]{:S(2)}) copy-start(f32[16]{0:T(128)S(1)} %get-tuple-element.419) | copy-start | bytes 196
  14.1 1.7 copy-start.27
  39.0 8.5 %copy-start.20 = (f32[32,1,1,16]{3,2,1,0:T(1,128)}, f32[32,1,1,16]{3,2,1,0:T(1,128)S(1)}, u32[]{:S(2)}) copy-start(f32[32,1,1,16]{3,2,1,0:T(1,128)S(1)} %all-gather) | copy-start | bytes 6148
  60.8 0.7 copy-start.33
  60.8 1.1 copy-start.10
  60.8 1.3 copy-start.11
  60.8 1.6 copy-start.5
  60.8 1.6 copy-start.6
  60.8 242.6 %all-gather.5.cloned.1.call-start = ((), (), s32[]{:S(2)}) async-start(), calls=%async_computation.2 | async-start | bytes 17301504 | tf_op jit(solution)/shard_map/all_gather | solution.py:15
  60.9 127.2 %copy-start.24 = (f32[1,256,1,16]{1,3,2,0:T(8,128)}, f32[1,256,1,16]{1,3,2,0:T(8,128)S(1)}, u32[]{:S(2)}) copy-start(f32[1,256,1,16]{1,3,2,0:T(8,128)S(1)} %copy.248) | copy-start | bytes 49156
  61.4 156.1 %copy-start.15 = (f32[1,256,1,16]{1,3,2,0:T(8,128)}, f32[1,256,1,16]{1,3,2,0:T(8,128)S(1)}, u32[]{:S(2)}) copy-start(f32[1,256,1,16]{1,3,2,0:T(8,128)S(1)} %copy.254) | copy-start | bytes 49156
  61.8 152.8 %copy-start.18 = (f32[1024]{0:T(1024)}, f32[1024]{0:T(1024)S(1)}, u32[]{:S(2)}) copy-start(f32[1024]{0:T(1024)S(1)} %mul.544) | copy-start | bytes 12292
  62.0 126.1 %copy-start.1 = (bf16[256,1024]{0,1:T(8,128)(2,1)}, bf16[256,1024]{0,1:T(8,128)(2,1)S(1)}, u32[]{:S(2)}) copy-start(bf16[256,1024]{0,1:T(8,128)(2,1)S(1)} %copy.255) | copy-start | bytes 1572868
  184.8 3.7 copy-start.3
  184.8 18.3 %copy-start.23 = (f32[1024]{0:T(1024)S(1)}, f32[1024]{0:T(1024)}, u32[]{:S(2)}) copy-start(f32[1024]{0:T(1024)} %param.21) | copy-start | bytes 12292
  188.1 1.0 copy-start.2
  217.5 6.9 %copy-start.4 = (bf16[256,1024]{0,1:T(8,128)(2,1)S(1)}, bf16[256,1024]{0,1:T(8,128)(2,1)}, u32[]{:S(2)}) copy-start(bf16[256,1024]{0,1:T(8,128)(2,1)} %get-tuple-element.412) | copy-start | bytes 1572868
  217.6 7.9 %copy-start = (f32[16,64,128]{2,1,0:T(8,128)S(1)}, f32[16,64,128]{2,1,0:T(8,128)}, u32[]{:S(2)}) copy-start(f32[16,64,128]{2,1,0:T(8,128)} %reduce-scatter.2.cloned.1.call-done) | copy-start | bytes 1572868
  228.6 134.1 %copy-start.7 = (bf16[256,128]{1,0:T(8,128)(2,1)S(1)}, bf16[256,128]{1,0:T(8,128)(2,1)}, u32[]{:S(2)}) copy-start(bf16[256,128]{1,0:T(8,128)(2,1)} %param.16) | copy-start | bytes 196612
  303.4 62.8 %copy-start.17 = (f32[256,16]{0,1:T(8,128)S(1)}, f32[256,16]{0,1:T(8,128)}, u32[]{:S(2)}) copy-start(f32[256,16]{0,1:T(8,128)} %param.15) | copy-start | bytes 49156
  303.4 62.8 %copy-start.28 = (f32[256]{0:T(256)S(1)}, f32[256]{0:T(256)}, u32[]{:S(2)}) copy-start(f32[256]{0:T(256)} %copy-done.27) | copy-start | bytes 3076
  303.4 62.8 %copy-start.31 = (f32[16]{0:T(128)S(1)}, f32[16]{0:T(128)}, u32[]{:S(2)}) copy-start(f32[16]{0:T(128)} %param.18) | copy-start | bytes 196
  303.4 62.9 %copy-start.22 = (s32[256]{0:T(256)S(1)}, s32[256]{0:T(256)}, u32[]{:S(2)}) copy-start(s32[256]{0:T(256)} %copy-done.21) | copy-start | bytes 3076
  362.7 4.1 %copy-start.8 = (f32[256,1,16,64]{0,3,2,1:T(8,128)S(1)}, f32[256,1,16,64]{0,3,2,1:T(8,128)}, u32[]{:S(2)}) copy-start(f32[256,1,16,64]{0,3,2,1:T(8,128)} %convert.11) | copy-start | bytes 3145732
  362.7 4.1 %copy-start.25 = (f32[1,256,1,16]{1,3,2,0:T(8,128)S(1)}, f32[1,256,1,16]{1,3,2,0:T(8,128)}, u32[]{:S(2)}) copy-start(f32[1,256,1,16]{1,3,2,0:T(8,128)} %copy-done.24) | copy-start | bytes 49156
  364.3 2.5 copy-start.16
  366.3 8.9 %copy-start.26 = (f32[256,1,16]{0,2,1:T(8,128)}, f32[256,1,16]{0,2,1:T(8,128)S(1)}, u32[]{:S(2)}) copy-start(f32[256,1,16]{0,2,1:T(8,128)S(1)} %get-tuple-element.299) | copy-start | bytes 49156
  366.4 8.8 %copy-start.13 = (f32[256,256]{1,0:T(8,128)}, f32[256,256]{1,0:T(8,128)S(1)}, u32[]{:S(2)}) copy-start(f32[256,256]{1,0:T(8,128)S(1)} %fusion.81) | copy-start | bytes 786436
  366.8 8.4 %copy-start.14 = (f32[256,256]{1,0:T(8,128)}, f32[256,256]{1,0:T(8,128)S(1)}, u32[]{:S(2)}) copy-start(f32[256,256]{1,0:T(8,128)S(1)} %fusion.85) | copy-start | bytes 786436
  366.9 9.4 %copy-start.12 = (f32[1,256,1,16]{3,2,1,0:T(1,128)S(1)}, f32[1,256,1,16]{3,2,1,0:T(1,128)}, u32[]{:S(2)}) copy-start(f32[1,256,1,16]{3,2,1,0:T(1,128)} %copy.259) | copy-start | bytes 49156
  376.3 15.7 %copy-start.9 = (f32[256,16,64]{0,2,1:T(8,128)S(1)}, f32[256,16,64]{0,2,1:T(8,128)}, u32[]{:S(2)}) copy-start(f32[256,16,64]{0,2,1:T(8,128)} %get-tuple-element.426) | copy-start | bytes 3145732
  389.3 7.5 %copy-start.19 = (f32[1024]{0:T(1024)S(1)}, f32[1024]{0:T(1024)}, u32[]{:S(2)}) copy-start(f32[1024]{0:T(1024)} %copy-done.18) | copy-start | bytes 12292
Sparse Core Ops, SparseCore 0:
  60.9 122.2 reduce-scatter.1
  219.1 84.1 all-gather.4
where the time goes:
time: 408 us; the launch traced here: 405 us
  waiting for transfers between devices  195 us (48%)
  other arithmetic  72.1 us (18%)
  blocking collectives  48.4 us (12%)
  local copies, waits for them, and re-layouts  40.9 us (10%)
  matrix products  31.2 us (8%)
  between operations  15.9 us (4%)
    reduce_scatter x1, waiting for transfers between devices, body(): lax.psum_scatter(weight[:, None, None] * jnp.take(flat_end, head_ids, axi...  121 us
    all_gather x1, waiting for transfers between devices, carried_in(): everything = jax.tree.map(lambda part: lax.all_gather(part, axis), array)  74.7 us
    select_n x32, other arithmetic, turn(): return jax.tree.map(lambda a, b: jnp.where(reached, a, b), new, before)  37.4 us
    all_gather x1, blocking collectives, body(): decay_table = lax.all_gather(through_all, 'ctx', axis=0, tiled=True)  23.2 us
    mul x32, local copies, waits for them, and re-layouts, compose(): decay_late[..., None, None] * sum_early + sum_late  21.1 us
    dot_general x3, matrix products, span_mix(): jnp.einsum('ghts,sghp->tghp', weights, x_span, precision=HIGHEST_PRECISION)  16.4 us
    psum x1, blocking collectives, body(): squares = lax.psum(jnp.sum(gated * gated, axis=1), 'head')  14 us
    mul x1, other arithmetic, body(): weight[:, None, None] * jnp.take(flat_end, head_ids, axis=0)  11.9 us
  transfers between devices with their start and end apart: 2, of which 2 were waited for; matrix products, arithmetic and copies ran while one was open for 3% of the time, Pallas kernels for 0%

commit v1 on v0

--- a/solution.py
+++ b/solution.py
@@ -135,7 +135,9 @@
 
     (starts, end_local, through_all), states_back = jax.vjp(states_call, x_spans, dt_spans, b_spans)
     identity = (jnp.ones_like(through_all), jnp.zeros_like(end_local))
-    decay_table = lax.all_gather(through_all, "ctx", axis=0, tiled=True)
+    decay_table = jnp.concatenate(
+        lax.all_to_all(jnp.stack([through_all] * lax.axis_size("ctx")), "ctx", 0, 0), axis=0
+    )
     own_index = lax.axis_index("ctx")
     ctx_count = lax.axis_size("ctx")
     flat_end = end_local.reshape(heads_here, HEAD_DIM, STATE)

time: 408 us -> 380 us (0.931)
  waiting for transfers between devices: 195 us -> 157 us
  starting transfers between devices: 0.08 us -> 8.66 us
  blocking collectives: 48.4 us -> 56.8 us
    all_gather x1, waiting for transfers between devices: 74.7 us -> 34.9 us  [carried_in(): everything = jax.tree.map(lambda part: lax.all_gather(part, axis), array)]
    all_to_all x0 -> x1, starting transfers between devices: none -> 8.58 us  [body(): lax.all_to_all(jnp.stack([through_all] * lax.axis_size('ctx')), 'ctx', 0, 0)]
    all_gather x1, blocking collectives: 23.2 us -> 31.5 us  [carried_in(): everything = jax.tree.map(lambda part: lax.all_gather(part, axis), array)]
  transfers between devices with their start and end apart: 2 -> 3, of which waited for: 2 -> 2; matrix products, arithmetic and copies ran while one was open for 3% -> 8% of each run, Pallas kernels for 0% -> 0%
where the time goes in v1:
time: 380 us; the launch traced here: 377 us
  waiting for transfers between devices  157 us (41%)
  other arithmetic  69.8 us (18%)
  blocking collectives  56.8 us (15%)
  local copies, waits for them, and re-layouts  37 us (10%)
  matrix products  30.8 us (8%)
  between operations  15.9 us (4%)
  starting transfers between devices  8.66 us (2%)
    reduce_scatter x1, waiting for transfers between devices, body(): lax.psum_scatter(weight[:, None, None] * jnp.take(flat_end, head_ids, axi...  123 us
    select_n x32, other arithmetic, turn(): return jax.tree.map(lambda a, b: jnp.where(reached, a, b), new, before)  37.4 us
    all_gather x1, waiting for transfers between devices, carried_in(): everything = jax.tree.map(lambda part: lax.all_gather(part, axis), array)  34.9 us
    all_gather x1, blocking collectives, carried_in(): everything = jax.tree.map(lambda part: lax.all_gather(part, axis), array)  31.5 us
    mul x32, local copies, waits for them, and re-layouts, compose(): decay_late[..., None, None] * sum_early + sum_late  20.4 us
    dot_general x3, matrix products, span_mix(): jnp.einsum('ghts,sghp->tghp', weights, x_span, precision=HIGHEST_PRECISION)  17.4 us
    psum x1, blocking collectives, body(): squares = lax.psum(jnp.sum(gated * gated, axis=1), 'head')  13.9 us
    mul x1, other arithmetic, body(): weight[:, None, None] * jnp.take(flat_end, head_ids, axis=0)  11.9 us
  transfers between devices with their start and end apart: 3, of which 2 were waited for; matrix products, arithmetic and copies ran while one was open for 8% of the time, Pallas kernels for 0%

profile of v1, /device:TPU:1, one launch (start us, length us, event | category | flops | bytes accessed | tf_op | source)
XLA Modules:
  0.0 377.4 jit_solution(2483100314060556413)
XLA Ops:
  7.8 1.4 fusion.113
  10.0 1.0 reduce-window.30
  15.7 8.6 %all-to-all-start = ((f32[32,1,16]{2,1,0:T(1,128)}), f32[32,1,16]{2,1,0:T(1,128)S(1)}, u32[]{:S(2)}, u32[]{:S(2)}) async-start(f32[32,1,16]{2,1,0:T(1,128)} %stack.2), calls=%async_computation | async-start | bytes 32768 | tf_op jit(solution)/shard_map/all_to_all | solution.py:139
  25.2 1.2 copy.113
  26.5 1.5 fusion.46
  28.0 7.0 %gather_fusion.1 = f32[512,64,128]{2,1,0:T(8,128)} fusion(f32[16,64,128]{2,1,0:T(8,128)S(1)} %fusion.46, s32[1024]{0:T(1024)S(1)} %pad_clamp_fusion), kind=kCustom, calls=%fused_computation.1 | custom fusion | bytes 33556480 | tf_op jit(solution)/shard_map/jit(_take)/gather | solution.py:152
  35.0 1.0 gather_fusion
  36.3 11.9 %select_multiply_fusion = f32[512,64,128]{2,1,0:T(8,128)} fusion(f32[512,64,128]{2,1,0:T(8,128)} %gather_fusion.1, f32[512]{0:T(512)S(1)} %compare_select_fusion.3, pred[512]{0:T(512)(128)(4,1)S(1)} %compare_and_fusion), kind=kLoop, calls=%fused_computation.5 | loop fusion | flops 8388608 | bytes 33556992 | tf_op jit(solution)/shard_map/mul | solution.py:152
  50.0 122.6 %reduce-scatter.2.cloned.1.call-done = f32[16,64,128]{2,1,0:T(8,128)} async-done(((f32[512,64,128]{2,1,0:T(8,128)}), f32[16,64,128]{2,1,0:T(8,128)}) %reduce-scatter.2.cloned.1.call-update) | async-done | bytes 524304 | tf_op jit(solution)/shard_map/reduce_scatter | solution.py:151
  172.7 1.6 convolution_bitcast_fusion.1
  174.3 3.2 fusion.38
  178.5 13.9 %psum.14 = f32[256]{0:T(256)S(1)} all-reduce(f32[256]{0:T(256)S(1)} %get-tuple-element.388), channel_id=1, replica_groups=mesh['ctx'=32,'head'=8] {'head'}, use_global_device_ids=true, to_apply=%region_7.8 | all-reduce | flops 256 | bytes 2048 | tf_op jit(solution)/shard_map/psum | solution.py:173
  192.7 11.3 %psum.15 = f32[256]{0:T(256)S(1)} all-reduce(f32[256]{0:T(256)S(1)} %multiply_reduce_fusion.1), channel_id=1, replica_groups=mesh['ctx'=32,'head'=8] {'head'}, use_global_device_ids=true, to_apply=%region_9.10 | all-reduce | flops 256 | bytes 2048 | tf_op jit(solution)/shard_map/psum | solution.py:176
  204.1 3.2 fusion.56
  207.3 1.4 fusion.58
  208.8 1.1 convert.11
  209.9 31.5 %all-gather = f32[32,1,1,16]{3,2,1,0:T(1,128)} all-gather(f32[1,1,1,16]{3,2,1,0:T(1,128)S(1)} %copy.123), channel_id=2, replica_groups=mesh['ctx'=32,'head'=8] {'ctx'}, dimensions={0}, use_global_device_ids=true | all-gather | bytes 2112 | tf_op jit(solution)/shard_map/all_gather | solution.py:15
  241.5 1.0 copy.139
  242.5 2.6 convolution_bitcast_fusion.3
  245.1 1.4 multiply_reduce_fusion
  247.8 9.1 %fusion.77 = (f32[16,256]{1,0:T(8,128)}, f32[16,256]{1,0:T(8,128)}, f32[16,256]{1,0:T(8,128)}, f32[256,256]{1,0:T(8,128)S(1)}) fusion(f32[16,256]{1,0:T(8,128)S(1)} %bitcast.286, f32[256,256]{1,0:T(8,128)S(1)} %fusion.81, f32[16,256]{1,0:T(8,128)} %bitcast.296, f32[256,256]{1,0:T(8,128)S(1)} %fusion.84, f32[256,1,16,64]{0,3,2,1:T(8,128)S(1)} %copy-done.8, ...), kind=kOutput, calls=%fused_computation.95 | convolution fusion | flops 825151488 | bytes 2965504 | tf_op jit(solution)/shard_map/transpose(jvp())/while/body/eval_jaxpr/checkpoint/ghts,sghp->tghp/dot_general | solution.py:41
  256.8 1.0 convolution_add_fusion
  257.9 34.9 %all-gather.4.cloned.1.call-done = f32[512,64,128]{2,1,0:T(8,128)} async-done(((f32[16,64,128]{2,1,0:T(8,128)}), f32[512,64,128]{2,1,0:T(8,128)}) %all-gather.4.cloned.1.call-update) | async-done | bytes 16777232 | tf_op jit(solution)/shard_map/all_gather | solution.py:15
  292.7 58.8 %while.11 = (s32[]{:T(128)}, f32[1,16,64,128]{3,2,1,0:T(8,128)S(1)}, s32[]{:T(128)}, f32[32,1,16]{2,1,0:T(1,128)}, f32[32,1,16,64,128]{4,3,2,1,0:T(8,128)}, /*index=5*/s32[]{:T(128)}, s32[]{:T(128)}, s32[]{:T(128)}, s32[]{:T(128)}) while((s32[]{:T(128)}, f32[1,16,64,128]{3,2,1,0:T(8,128)S(1)}, s32[]{:T(128)}, ...), condition=%wide.region_11.12_spmd.clone, body=%wide.region_10.11_spmd.clone.sunk | while | flops 524296 | bytes 1573231 | solution.py:28
  293.3 1.2 fusion.126
  295.2 1.2 fusion.126
  297.1 1.2 fusion.126
  298.9 1.2 fusion.126
  300.7 1.2 fusion.126
  302.5 1.2 fusion.126
  304.3 1.2 fusion.126
  306.1 1.2 fusion.126
  308.0 1.2 fusion.126
  309.9 1.2 fusion.126
  311.7 1.2 fusion.126
  313.6 1.2 fusion.126
  315.4 1.2 fusion.126
  317.3 1.2 fusion.126
  319.1 1.2 fusion.126
  320.9 1.2 fusion.126
  322.7 1.2 fusion.126
  324.6 1.2 fusion.126
  326.4 1.2 fusion.126
  328.2 1.2 fusion.126
  330.1 1.2 fusion.126
  331.9 1.2 fusion.126
  333.7 1.2 fusion.126
  335.6 1.2 fusion.126
  337.4 1.2 fusion.126
  339.3 1.2 fusion.126
  341.1 1.2 fusion.126
  342.9 1.2 fusion.126
  344.8 1.2 fusion.126
  346.7 1.2 fusion.126
  348.5 1.2 fusion.126
  350.4 1.2 fusion.126
  351.6 1.8 fusion.47
  353.4 1.6 fusion.50
  355.4 1.0 fusion.115
  356.5 2.5 reduce-window.36
  359.1 2.5 reduce-window.34
  361.7 1.3 fusion.49
  363.0 5.1 %fusion.41 = f32[256,16,64]{0,2,1:T(8,128)S(1)} fusion(f32[16,256]{1,0:T(8,128)} %bitcast.297, f32[256,256]{1,0:T(8,128)S(1)} %copy-done.13, f32[16,256]{1,0:T(8,128)S(1)} %bitcast.288, f32[256,256]{1,0:T(8,128)} %copy-done.14, f32[256,1,16,64]{0,3,2,1:T(8,128)S(1)} %bitcast.279, f32[256,16,64]{0,2,1:T(8,128)} %get-tuple-element.406, ...), kind=kOutput, calls=%fused_computation.47 | convolution fusion | flops 811073536 | bytes 3719168 | tf_op jit(solution)/shard_map/transpose(jvp())/while/body/eval_jaxpr/checkpoint/ghts,sghp->tghp/dot_general | solution.py:41
  368.3 1.0 copy.138
  (171 shorter events, 32.9 us)
Async XLA Ops:
  7.8 1.4 copy-start.29
  12.0 2.2 copy-start.27
  12.0 37.7 %copy-start.20 = (s32[256]{0:T(256)}, s32[256]{0:T(256)S(1)}, u32[]{:S(2)}) copy-start(s32[256]{0:T(256)S(1)} %get-tuple-element.298) | copy-start | bytes 3076
  14.2 193.0 %copy-start.17 = (f32[256,16]{0,1:T(8,128)}, f32[256,16]{0,1:T(8,128)S(1)}, u32[]{:S(2)}) copy-start(f32[256,16]{0,1:T(8,128)S(1)} %get-tuple-element.390) | copy-start | bytes 49156
  15.0 19.9 %copy-start.25 = (f32[16]{0:T(128)}, f32[16]{0:T(128)S(1)}, u32[]{:S(2)}) copy-start(f32[16]{0:T(128)S(1)} %get-tuple-element.404) | copy-start | bytes 196
  15.7 19.3 %all-to-all-start = ((f32[32,1,16]{2,1,0:T(1,128)}), f32[32,1,16]{2,1,0:T(1,128)S(1)}, u32[]{:S(2)}, u32[]{:S(2)}) async-start(f32[32,1,16]{2,1,0:T(1,128)} %stack.2), calls=%async_computation | async-start | bytes 32768 | tf_op jit(solution)/shard_map/all_to_all | solution.py:139
  24.3 148.4 %reduce-scatter.2.cloned.1.call-start = ((), (), s32[]{:S(2)}) async-start(), calls=%async_computation.2 | async-start | bytes 17301504 | tf_op jit(solution)/shard_map/reduce_scatter | solution.py:151
  24.4 10.6 %copy-start.22 = (f32[256]{0:T(256)}, f32[256]{0:T(256)S(1)}, u32[]{:S(2)}) copy-start(f32[256]{0:T(256)S(1)} %compare_convert_fusion.1) | copy-start | bytes 3076
  25.2 9.8 %copy-start.15 = (f32[256,16]{0,1:T(8,128)}, f32[256,16]{0,1:T(8,128)S(1)}, u32[]{:S(2)}) copy-start(f32[256,16]{0,1:T(8,128)S(1)} %fusion.98) | copy-start | bytes 49156
  48.2 0.7 copy-start.31
  48.2 1.1 copy-start.9
  48.2 1.3 copy-start.10
  48.2 1.6 copy-start.6
  48.2 1.6 copy-start.7
  48.3 244.5 %all-gather.4.cloned.1.call-start = ((), (), s32[]{:S(2)}) async-start(), calls=%async_computation.3 | async-start | bytes 17301504 | tf_op jit(solution)/shard_map/all_gather | solution.py:15
  49.3 154.8 %copy-start.18 = (f32[1024]{0:T(1024)}, f32[1024]{0:T(1024)S(1)}, u32[]{:S(2)}) copy-start(f32[1024]{0:T(1024)S(1)} %mul.534) | copy-start | bytes 12292
  49.5 128.0 %copy-start.2 = (bf16[256,1024]{0,1:T(8,128)(2,1)}, bf16[256,1024]{0,1:T(8,128)(2,1)S(1)}, u32[]{:S(2)}) copy-start(bf16[256,1024]{0,1:T(8,128)(2,1)S(1)} %copy.120) | copy-start | bytes 1572868
  49.7 142.7 %copy-start.1 = (bf16[256,1024]{0,1:T(8,128)(2,1)}, bf16[256,1024]{0,1:T(8,128)(2,1)S(1)}, u32[]{:S(2)}) copy-start(bf16[256,1024]{0,1:T(8,128)(2,1)S(1)} %copy.121) | copy-start | bytes 1572868
  174.3 3.7 copy-start.4
  174.3 18.2 %copy-start.21 = (f32[1024]{0:T(1024)S(1)}, f32[1024]{0:T(1024)}, u32[]{:S(2)}) copy-start(f32[1024]{0:T(1024)} %param.21) | copy-start | bytes 12292
  177.5 1.0 copy-start.3
  204.1 38.4 %copy-start = (f32[16,64,128]{2,1,0:T(8,128)S(1)}, f32[16,64,128]{2,1,0:T(8,128)}, u32[]{:S(2)}) copy-start(f32[16,64,128]{2,1,0:T(8,128)} %reduce-scatter.2.cloned.1.call-done) | copy-start | bytes 1572868
  207.3 34.2 %copy-start.5 = (bf16[256,1024]{0,1:T(8,128)(2,1)S(1)}, bf16[256,1024]{0,1:T(8,128)(2,1)}, u32[]{:S(2)}) copy-start(bf16[256,1024]{0,1:T(8,128)(2,1)} %get-tuple-element.396) | copy-start | bytes 1572868
  242.5 5.3 %copy-start.8 = (f32[256,1,16,64]{0,3,2,1:T(8,128)S(1)}, f32[256,1,16,64]{0,3,2,1:T(8,128)}, u32[]{:S(2)}) copy-start(f32[256,1,16,64]{0,3,2,1:T(8,128)} %convert.11) | copy-start | bytes 3145732
  247.3 9.5 %copy-start.12 = (f32[256,256]{1,0:T(8,128)}, f32[256,256]{1,0:T(8,128)S(1)}, u32[]{:S(2)}) copy-start(f32[256,256]{1,0:T(8,128)S(1)} %fusion.81) | copy-start | bytes 786436
  247.7 9.1 %copy-start.14 = (f32[256,256]{1,0:T(8,128)}, f32[256,256]{1,0:T(8,128)S(1)}, u32[]{:S(2)}) copy-start(f32[256,256]{1,0:T(8,128)S(1)} %fusion.84) | copy-start | bytes 786436
  257.9 93.7 %copy-start.16 = (f32[256,16]{0,1:T(8,128)S(1)}, f32[256,16]{0,1:T(8,128)}, u32[]{:S(2)}) copy-start(f32[256,16]{0,1:T(8,128)} %copy-done.15) | copy-start | bytes 49156
  351.5 3.8 %copy-start.11 = (f32[256,16]{0,1:T(8,128)S(1)}, f32[256,16]{0,1:T(8,128)}, u32[]{:S(2)}) copy-start(f32[256,16]{0,1:T(8,128)} %param.15) | copy-start | bytes 49156
  351.6 11.4 %copy-start.13 = (f32[256,256]{1,0:T(8,128)S(1)}, f32[256,256]{1,0:T(8,128)}, u32[]{:S(2)}) copy-start(f32[256,256]{1,0:T(8,128)} %copy-done.12) | copy-start | bytes 786436
  355.2 12.9 %copy-start.19 = (f32[1024]{0:T(1024)S(1)}, f32[1024]{0:T(1024)}, u32[]{:S(2)}) copy-start(f32[1024]{0:T(1024)} %copy-done.18) | copy-start | bytes 12292
  363.0 6.8 %copy-start.23 = (f32[256]{0:T(256)S(1)}, f32[256]{0:T(256)}, u32[]{:S(2)}) copy-start(f32[256]{0:T(256)} %copy-done.22) | copy-start | bytes 3076
  363.0 6.8 %copy-start.24 = (f32[16,256]{1,0:T(8,128)S(1)}, f32[16,256]{1,0:T(8,128)}, u32[]{:S(2)}) copy-start(f32[16,256]{1,0:T(8,128)} %get-tuple-element.372) | copy-start | bytes 49156
  363.0 6.8 %copy-start.26 = (f32[16]{0:T(128)S(1)}, f32[16]{0:T(128)}, u32[]{:S(2)}) copy-start(f32[16]{0:T(128)} %copy-done.25) | copy-start | bytes 196
  363.0 6.9 %copy-start.28 = (f32[16]{0:T(128)S(1)}, f32[16]{0:T(128)}, u32[]{:S(2)}) copy-start(f32[16]{0:T(128)} %param.18) | copy-start | bytes 196
  363.0 6.8 %copy-start.30 = (f32[16]{0:T(128)S(1)}, f32[16]{0:T(128)}, u32[]{:S(2)}) copy-start(f32[16]{0:T(128)} %copy-done.29) | copy-start | bytes 196
Sparse Core Ops, SparseCore 0:
  48.4 124.2 reduce-scatter.1
  208.8 83.8 all-gather.3
